TPU v7x, 256 devices: a whole 4x4x8 slice. The times are simulated.
256 devices in a mesh: var: 8 (over y, core), tok: 32 (over x, z).
Axes of the slice: x: 4, y: 4, z: 8, core: 2. Of those that a mesh axis runs over, the one named last changes fastest.
Arguments:
- patches: bfloat16 [72, 4, 4096], P('var', None, 'tok'), may hold values from -6 to 6
- slot_var: int32 [72], replicated, may hold values from -1 to 47, as said below
- patch_weight: bfloat16 [48, 4, 1024], replicated, may hold values from -3 to 3
- var_embed: bfloat16 [48, 1024], replicated, may hold values from -6 to 6
- query: bfloat16 [1024], replicated, may hold values from -16 to 16
- key_weight: bfloat16 [1024, 1024], P('tok'), may hold values from -0.1875 to 0.1875
- value_weight: bfloat16 [1024, 1024], P('tok'), may hold values from -0.1875 to 0.1875
- out_weight: bfloat16 [1024, 1024], P('tok'), may hold values from -0.1875 to 0.1875
- cotangent: bfloat16 [4096, 1024], P(('tok', 'var')), may hold values from -6 to 6
Outputs:
- aggregated: bfloat16 [4096, 1024], P(('tok', 'var'))
- patch_grad: float32 [72, 4096], P('var', 'tok')
Inputs may be any that keep to these rules, and one draw needn't show every extreme that they name: `slot_var`: slot 9 * i + j belongs to index i of var. Every variable id stands in exactly one slot; empty slots hold -1. The live slots of an index come first and hold consecutive ids, rising from index to index. Every index holds at least one and at most 9 live slots, and some index holds exactly 9.
All inputs are finite; a program needn't handle non-finite values.
Results may differ from a plain program's by a relative error of at most 0.011.
Values may be sent and summed in bfloat16 or wider, within the bound.
No kernel may reach another device: no remote copies, remote signals or barrier semaphores. Data moves between devices by JAX's collectives and lax.ppermute only.
A program may use at most 128 MiB of HBM per device.

v0:
```python
import math
import jax
import jax.numpy as jnp
from jax import lax
from jax.sharding import PartitionSpec as P

H = 16
HD = 64
score_cap = 5.0
inv_sqrt_two = 1.0 / math.sqrt(2.0)
inv_sqrt_two_pi = 1.0 / math.sqrt(2.0 * math.pi)


def gelu_exact(inputs):
    return 0.5 * inputs * (1.0 + lax.erf(inputs * inv_sqrt_two))


def gelu_slope(inputs):
    return (
        0.5 * (1.0 + lax.erf(inputs * inv_sqrt_two))
        + inputs * jnp.exp(-0.5 * inputs * inputs) * inv_sqrt_two_pi
    )


def live_index(slot_var, var_total):
    ids = jnp.arange(var_total, dtype=jnp.int32)
    places = jnp.arange(slot_var.shape[0], dtype=jnp.int32)
    match = slot_var[None, :] == ids[:, None]
    return jnp.sum(jnp.where(match, places[None, :], 0), axis=1)


def attend(embedded, query, key_matrix, value_matrix, out_matrix, cot_rows):
    var_count, tok_count, width = embedded.shape
    flat_rows = embedded.reshape(var_count * tok_count, width)
    key_heads = (
        jnp.dot(flat_rows, key_matrix, preferred_element_type=jnp.float32)
        .astype(jnp.bfloat16)
        .reshape(var_count, tok_count, H, HD)
    )
    value_heads = (
        jnp.dot(flat_rows, value_matrix, preferred_element_type=jnp.float32)
        .astype(jnp.bfloat16)
        .reshape(var_count, tok_count, H, HD)
    )
    query_heads = query.reshape(H, HD)
    raw_scores = jnp.einsum(
        "vthj,hj->tvh", key_heads, query_heads, preferred_element_type=jnp.float32
    ) / math.sqrt(HD)
    squashed = jnp.tanh(raw_scores / score_cap)
    exp_scores = jnp.exp(score_cap * squashed)
    attn_f32 = exp_scores / jnp.sum(exp_scores, axis=1, keepdims=True)
    attn_bf = attn_f32.astype(jnp.bfloat16)
    pooled = (
        jnp.einsum("tvh,vthj->thj", attn_bf, value_heads, preferred_element_type=jnp.float32)
        .astype(jnp.bfloat16)
        .reshape(tok_count, width)
    )
    mixed_out = jnp.dot(pooled, out_matrix, preferred_element_type=jnp.float32).astype(jnp.bfloat16)
    contract = (((1,), (1,)), ((), ()))
    grad_pooled = (
        lax.dot_general(cot_rows, out_matrix, contract, preferred_element_type=jnp.float32)
        .astype(jnp.bfloat16)
        .reshape(tok_count, H, HD)
    )
    grad_attn = jnp.einsum(
        "thj,vthj->tvh", grad_pooled, value_heads, preferred_element_type=jnp.float32
    )
    attn_vth = jnp.transpose(attn_bf, (1, 0, 2)).astype(jnp.float32)
    grad_values = (attn_vth[:, :, :, None] * grad_pooled.astype(jnp.float32)[None]).astype(
        jnp.bfloat16
    )
    grad_scores = attn_f32 * (grad_attn - jnp.sum(attn_f32 * grad_attn, axis=1, keepdims=True))
    grad_raw = grad_scores * (1.0 - squashed * squashed) / math.sqrt(HD)
    query_f32 = query_heads.astype(jnp.float32)
    grad_keys = (jnp.transpose(grad_raw, (1, 0, 2))[:, :, :, None] * query_f32[None, None]).astype(
        jnp.bfloat16
    )
    grad_embed = lax.dot_general(
        grad_keys.reshape(var_count * tok_count, width),
        key_matrix,
        contract,
        preferred_element_type=jnp.float32,
    )
    grad_embed = grad_embed + lax.dot_general(
        grad_values.reshape(var_count * tok_count, width),
        value_matrix,
        contract,
        preferred_element_type=jnp.float32,
    )
    return (mixed_out, grad_embed.astype(jnp.bfloat16).reshape(var_count, tok_count, width))


def body(
    patches,
    slot_var,
    patch_weight,
    var_embed,
    query,
    key_weight,
    value_weight,
    out_weight,
    cotangent,
):
    var_total, _, width = patch_weight.shape
    local_slots = patches.shape[0]
    live_slot = live_index(slot_var, var_total)
    key_matrix, value_matrix = (
        lax.all_gather(key_weight, "tok", axis=0, tiled=True),
        lax.all_gather(value_weight, "tok", axis=0, tiled=True),
    )
    out_matrix = lax.all_gather(out_weight, "tok", axis=0, tiled=True)
    first_slot = lax.axis_index("var") * local_slots
    own_vars = lax.dynamic_slice_in_dim(slot_var, first_slot, local_slots)
    picker = (own_vars[:, None] == jnp.arange(var_total, dtype=jnp.int32)[None, :]).astype(
        jnp.bfloat16
    )
    slot_table = (
        jnp.dot(
            picker, patch_weight.reshape(var_total, 4 * width), preferred_element_type=jnp.float32
        )
        .astype(jnp.bfloat16)
        .reshape(local_slots, 4, width)
    )
    slot_shift = jnp.dot(picker, var_embed, preferred_element_type=jnp.float32)
    pre_act = (
        jnp.einsum("spt,spd->std", patches, slot_table, preferred_element_type=jnp.float32)
        + slot_shift[:, None, :]
    )
    embedded = gelu_exact(pre_act).astype(jnp.bfloat16)
    spread = lax.all_to_all(embedded, "var", split_axis=1, concat_axis=0, tiled=True)
    live_rows = jnp.take(spread, live_slot, axis=0)
    mixed_out, grad_embed = attend(
        live_rows, query, key_matrix, value_matrix, out_matrix, cotangent
    )
    grad_slots = jnp.zeros(spread.shape, jnp.bfloat16).at[live_slot].set(grad_embed)
    returned = lax.all_to_all(grad_slots, "var", split_axis=0, concat_axis=1, tiled=True)
    grad_pre = returned.astype(jnp.float32) * gelu_slope(pre_act)
    slot_grad = jnp.einsum(
        "spt,std->spd", patches.astype(jnp.float32), grad_pre, precision=lax.Precision.HIGHEST
    ).reshape(local_slots, 4 * width)
    grad_out = lax.psum_scatter(slot_grad, "tok", scatter_dimension=1, tiled=True)
    return (mixed_out, grad_out)


def solution(mesh):
    return jax.shard_map(
        body,
        mesh=mesh,
        in_specs=(
            P("var", None, "tok"),
            P(),
            P(),
            P(),
            P(),
            P("tok", None),
            P("tok", None),
            P("tok", None),
            P(("tok", "var"), None),
        ),
        out_specs=(P(("tok", "var"), None), P("var", "tok")),
        check_vma=False,
    )
```

profile of v0, /device:TPU:8, one launch (start us, length us, event | category | flops | bytes accessed | tf_op | source)
XLA Modules:
  0.0 545.3 jit_solution(2519850298434397522)
XLA Ops:
  9.4 1.1 copy.47
  11.8 4.6 fusion.6
  16.3 6.6 %copy.29 = bf16[9,128,1024]{2,0,1:T(8,128)(2,1)} copy(bf16[9,128,1024]{1,2,0:T(8,128)(2,1)S(1)} %get-tuple-element.6) | data formatting | bytes 4718592 | tf_op jit(solution)/shard_map/convert_element_type | solution.py:129
  22.9 6.7 %all-to-all-start = ((bf16[9,128,1024]{2,0,1:T(8,128)(2,1)}), bf16[9,128,1024]{2,0,1:T(8,128)(2,1)}, u32[]{:S(2)}, u32[]{:S(2)}) async-start(bf16[9,128,1024]{2,0,1:T(8,128)(2,1)} %copy.29), calls=%async_computation | async-start | bytes 8388608 | tf_op jit(solution)/shard_map/all_to_all | solution.py:130
  30.1 47.9 %all-to-all-done = bf16[9,128,1024]{2,0,1:T(8,128)(2,1)} async-done(((bf16[9,128,1024]{2,0,1:T(8,128)(2,1)}), bf16[9,128,1024]{2,0,1:T(8,128)(2,1)}, u32[]{:S(2)}, u32[]{:S(2)}) %all-to-all-start) | async-done | bytes 2359328 | tf_op jit(solution)/shard_map/all_to_all | solution.py:130
  78.0 3.7 copy.31
  81.7 1.9 gather_fusion
  83.6 1.6 bitcast_select_fusion
  85.3 6.1 %all-gather.8.cloned.1.call-done = bf16[1024,1024]{1,0:T(8,128)(2,1)} async-done(((bf16[32,1024]{1,0:T(8,128)(2,1)}), bf16[1024,1024]{1,0:T(8,128)(2,1)}) %all-gather.8.cloned.1.call-update) | async-done | bytes 2097168 | tf_op jit(solution)/shard_map/all_gather | solution.py:111
  91.4 2.2 convolution_convert_fusion.3
  93.9 75.1 %all-gather.6.cloned.1.call-done = bf16[1024,1024]{1,0:T(8,128)(2,1)} async-done(((bf16[32,1024]{1,0:T(8,128)(2,1)}), bf16[1024,1024]{1,0:T(8,128)(2,1)}) %all-gather.6.cloned.1.call-update) | async-done | bytes 2097168 | tf_op jit(solution)/shard_map/all_gather | solution.py:109
  168.9 4.6 convolution_convert_fusion.1
  173.5 4.1 reshape.85
  177.6 69.0 %all-gather.4.cloned.1.call-done = bf16[1024,1024]{1,0:T(8,128)(2,1)} async-done(((bf16[32,1024]{1,0:T(8,128)(2,1)}), bf16[1024,1024]{1,0:T(8,128)(2,1)}) %all-gather.4.cloned.1.call-update) | async-done | bytes 2097168 | tf_op jit(solution)/shard_map/all_gather | solution.py:108
  246.7 5.0 convolution_convert_fusion.2
  251.7 5.2 reshape.83
  256.9 5.3 fusion.12
  262.4 1.9 fusion.14
  264.9 3.8 mul.100
  268.8 6.3 %mul.101 = f32[768,1024]{1,0:T(8,128)} reshape(f32[48,16,16,64]{3,2,1,0:T(8,128)} %mul.100) | data formatting | bytes 6291456 | tf_op jit(solution)/shard_map/mul | solution.py:75
  276.1 3.3 multiply_convert_fusion
  279.4 3.2 convert_element_type.86
  282.6 4.5 fusion.22
  287.1 3.0 add_convert_fusion
  290.4 5.1 scatter_fusion
  295.5 33.5 %all_to_all.27 = bf16[72,16,1024]{2,1,0:T(8,128)(2,1)S(1)} all-to-all(bf16[72,16,1024]{2,1,0:T(8,128)(2,1)S(1)} %scatter_fusion), channel_id=1, replica_groups=mesh['var'=8,'tok'=32] {'var'}, dimensions={0} | all-to-all | bytes 4718592 | tf_op jit(solution)/shard_map/all_to_all | solution.py:136
  329.6 2.8 copy.34
  332.4 6.0 %copy.35 = f32[9,128,1024]{1,2,0:T(8,128)} copy(f32[9,128,1024]{2,1,0:T(8,128)} %bitcast.116) | data formatting | bytes 9437184 | tf_op jit(solution)/shard_map/convert_element_type | solution.py:137
  338.5 6.8 %fusion.24 = f32[9,4,1024]{2,1,0:T(4,128)S(1)} fusion(bf16[9,4,128]{2,1,0:T(4,128)(2,1)S(1)} %copy-done.7, f32[9,128,1024]{1,2,0:T(8,128)} %copy.35, f32[9,1024,128]{2,1,0:T(8,128)} %get-tuple-element.7, f32[9,1024]{1,0:T(8,128)S(1)} %fusion.30), kind=kOutput, calls=%fused_computation.36 | convolution fusion | flops 68419584 | bytes 9630720 | tf_op jit(solution)/shard_map/spt,std->spd/dot_general | solution.py:138
  346.3 3.8 fusion.16
  350.2 1.0 convolution_convert_fusion.4
  351.2 187.6 %reduce-scatter.2.cloned.1.call-done = f32[9,128]{1,0:T(8,128)} async-done(((f32[9,4096]{1,0:T(8,128)}), f32[9,128]{1,0:T(8,128)}) %reduce-scatter.2.cloned.1.call-update) | async-done | bytes 4624 | tf_op jit(solution)/shard_map/reduce_scatter | solution.py:141
  (56 shorter events, 7.7 us)
Async XLA Ops:
  7.2 4.4 copy-start
  7.2 84.2 %all-gather.8.cloned.1.call-start = ((), (), s32[]{:S(2)}) async-start(), calls=%async_computation.5 | async-start | bytes 2162688 | tf_op jit(solution)/shard_map/all_gather | solution.py:111
  7.9 161.0 %all-gather.6.cloned.1.call-start = ((), (), s32[]{:S(2)}) async-start(), calls=%async_computation.4 | async-start | bytes 2162688 | tf_op jit(solution)/shard_map/all_gather | solution.py:109
  8.7 238.0 %all-gather.4.cloned.1.call-start = ((), (), s32[]{:S(2)}) async-start(), calls=%async_computation.3 | async-start | bytes 2162688 | tf_op jit(solution)/shard_map/all_gather | solution.py:108
  22.9 6.7 %copy-start.8 = (bf16[1024]{0:T(1024)(128)(2,1)S(1)}, bf16[1024]{0:T(1024)(128)(2,1)}, u32[]{:S(2)}) copy-start(bf16[1024]{0:T(1024)(128)(2,1)} %param.13) | copy-start | bytes 6148
  22.9 6.8 %copy-start.10 = (s32[72]{0:T(128)S(1)}, s32[72]{0:T(128)}, u32[]{:S(2)}) copy-start(s32[72]{0:T(128)} %param.10) | copy-start | bytes 868
  22.9 55.1 %all-to-all-start = ((bf16[9,128,1024]{2,0,1:T(8,128)(2,1)}), bf16[9,128,1024]{2,0,1:T(8,128)(2,1)}, u32[]{:S(2)}, u32[]{:S(2)}) async-start(bf16[9,128,1024]{2,0,1:T(8,128)(2,1)} %copy.29), calls=%async_computation | async-start | bytes 8388608 | tf_op jit(solution)/shard_map/all_to_all | solution.py:130
  29.6 509.1 %reduce-scatter.2.cloned.1.call-start = ((), (), s32[]{:S(2)}) async-start(), calls=%async_computation.6 | async-start | bytes 270336 | tf_op jit(solution)/shard_map/reduce_scatter | solution.py:141
  81.7 9.7 %copy-start.6 = (bf16[16,1024]{1,0:T(8,128)(2,1)S(1)}, bf16[16,1024]{1,0:T(8,128)(2,1)}, u32[]{:S(2)}) copy-start(bf16[16,1024]{1,0:T(8,128)(2,1)} %param.17) | copy-start | bytes 98308
  85.2 83.7 %copy-start.4 = (bf16[768,1024]{1,0:T(8,128)(2,1)}, bf16[768,1024]{1,0:T(8,128)(2,1)S(1)}, u32[]{:S(2)}) copy-start(bf16[768,1024]{1,0:T(8,128)(2,1)S(1)} %bitcast_select_fusion) | copy-start | bytes 4718596
  177.6 84.8 %copy-start.3 = (bf16[48,16,16,64]{3,2,1,0:T(8,128)(2,1)}, bf16[48,16,16,64]{3,2,1,0:T(8,128)(2,1)S(1)}, u32[]{:S(2)}) copy-start(bf16[48,16,16,64]{3,2,1,0:T(8,128)(2,1)S(1)} %reshape.85) | copy-start | bytes 4718596
  282.6 4.5 copy-start.5
  282.6 4.5 copy-start.9
  332.4 6.1 %copy-start.7 = (bf16[9,4,128]{2,1,0:T(4,128)(2,1)S(1)}, bf16[9,4,128]{2,1,0:T(4,128)(2,1)}, u32[]{:S(2)}) copy-start(bf16[9,4,128]{2,1,0:T(4,128)(2,1)} %param.9) | copy-start | bytes 27652
  345.3 4.9 copy-start.2
  346.3 192.5 %copy-start.1 = (bf16[48,1024]{1,0:T(8,128)(2,1)S(1)}, bf16[48,1024]{1,0:T(8,128)(2,1)}, u32[]{:S(2)}) copy-start(bf16[48,1024]{1,0:T(8,128)(2,1)} %param.12) | copy-start | bytes 294916
Sparse Core Ops, SparseCore 0:
  10.6 80.7 all-gather.7
  94.0 74.9 all-gather.5
  171.5 75.0 all-gather.3
  346.4 192.3 reduce-scatter.1
where the time goes:
time: 546 us; the launch traced here: 545 us
  waiting for transfers between devices  388 us (71%)
  local copies, waits for them, and re-layouts  53.8 us (10%)
  matrix products  43.2 us (8%)
  blocking collectives  33.5 us (6%)
  between operations  14 us (3%)
  starting transfers between devices  6.85 us (1%)
  other arithmetic  6.17 us (1%)
    reduce_scatter x1, waiting for transfers between devices, body(): lax.psum_scatter(slot_grad, 'tok', scatter_dimension=1, tiled=True)  188 us
    all_gather x1, waiting for transfers between devices, body(): lax.all_gather(value_weight, 'tok', axis=0, tiled=True)  75.1 us
    all_gather x1, waiting for transfers between devices, body(): lax.all_gather(key_weight, 'tok', axis=0, tiled=True)  69 us
    all_to_all x1, waiting for transfers between devices, body(): lax.all_to_all(embedded, 'var', split_axis=1, concat_axis=0, tiled=True)  47.9 us
    all_to_all x1, blocking collectives, body(): lax.all_to_all(grad_slots, 'var', split_axis=0, concat_axis=1, tiled=True)  33.5 us
  transfers between devices with their start and end apart: 5, of which 5 were waited for; matrix products, arithmetic and copies ran while one was open for 7% of the time, Pallas kernels for 0%

commit v1 on v0

--- a/solution.py
+++ b/solution.py
@@ -1,3 +1,4 @@
+import functools
 import math
 import jax
 import jax.numpy as jnp
@@ -9,6 +10,17 @@
 score_cap = 5.0
 inv_sqrt_two = 1.0 / math.sqrt(2.0)
 inv_sqrt_two_pi = 1.0 / math.sqrt(2.0 * math.pi)
+
+
+def post_kinds(state, along_dim):
+    q_next = jnp.concatenate(
+        jax.lax.all_to_all(jnp.stack([state] * jax.lax.axis_size("tok"), axis=0), "tok", 0, 0),
+        axis=along_dim,
+    )
+    return q_next
+
+
+tell_levels_all = functools.partial(post_kinds, along_dim=0)
 
 
 def gelu_exact(inputs):
@@ -106,7 +118,7 @@
     live_slot = live_index(slot_var, var_total)
     key_matrix, value_matrix = (
         lax.all_gather(key_weight, "tok", axis=0, tiled=True),
-        lax.all_gather(value_weight, "tok", axis=0, tiled=True),
+        tell_levels_all(value_weight),
     )
     out_matrix = lax.all_gather(out_weight, "tok", axis=0, tiled=True)
     first_slot = lax.axis_index("var") * local_slots

time: 546 us -> 475 us (0.87)
  waiting for transfers between devices: 388 us -> 252 us
  blocking collectives: 33.5 us -> 89 us
    all_gather x1 -> x0, waiting for transfers between devices: 75.1 us -> none  [body(): lax.all_gather(value_weight, 'tok', axis=0, tiled=True)]
    all_to_all x0 -> x1, blocking collectives: none -> 55.5 us  [body(): lax.all_to_all(embedded, 'var', split_axis=1, concat_axis=0, tiled=True)]
    all_gather x1, waiting for transfers between devices: 69 us -> 23.7 us  [body(): lax.all_gather(key_weight, 'tok', axis=0, tiled=True)]
    all_to_all x1, waiting for transfers between devices: 47.9 us -> 39.6 us  [post_kinds(): jax.lax.all_to_all(jnp.stack([state] * jax.lax.axis_size('tok'), axis=0),...]
    all_gather x1, waiting for transfers between devices: 6.11 us -> 0.01 us  [body(): out_matrix = lax.all_gather(out_weight, 'tok', axis=0, tiled=True)]
  transfers between devices with their start and end apart: 5 -> 4, of which waited for: 5 -> 3; matrix products, arithmetic and copies ran while one was open for 7% -> 9% of each run, Pallas kernels for 0% -> 0%
where the time goes in v1:
time: 475 us; the launch traced here: 474 us
  waiting for transfers between devices  252 us (53%)
  blocking collectives  89 us (19%)
  local copies, waits for them, and re-layouts  57.3 us (12%)
  matrix products  44.8 us (9%)
  between operations  14 us (3%)
  starting transfers between devices  9.94 us (2%)
  other arithmetic  6.19 us (1%)
    reduce_scatter x1, waiting for transfers between devices, body(): lax.psum_scatter(slot_grad, 'tok', scatter_dimension=1, tiled=True)  188 us
    all_to_all x1, blocking collectives, body(): lax.all_to_all(embedded, 'var', split_axis=1, concat_axis=0, tiled=True)  55.5 us
    all_to_all x1, waiting for transfers between devices, post_kinds(): jax.lax.all_to_all(jnp.stack([state] * jax.lax.axis_size('tok'), axis=0),...  39.6 us
    all_to_all x1, blocking collectives, body(): lax.all_to_all(grad_slots, 'var', split_axis=0, concat_axis=1, tiled=True)  33.5 us
    all_gather x1, waiting for transfers between devices, body(): lax.all_gather(key_weight, 'tok', axis=0, tiled=True)  23.7 us
    mul x2, local copies, waits for them, and re-layouts, attend(): jnp.transpose(grad_raw, (1, 0, 2))[:, :, :, None] * query_f32[None, None]  10.1 us
    all_to_all x1, starting transfers between devices, post_kinds(): jax.lax.all_to_all(jnp.stack([state] * jax.lax.axis_size('tok'), axis=0),...  9.83 us
  transfers between devices with their start and end apart: 4, of which 3 were waited for; matrix products, arithmetic and copies ran while one was open for 9% of the time, Pallas kernels for 0%

profile of v1, /device:TPU:8, one launch (start us, length us, event | category | flops | bytes accessed | tf_op | source)
XLA Modules:
  0.0 473.5 jit_solution(12397407487997968455)
XLA Ops:
  7.9 1.1 copy.47
  10.3 4.5 fusion.6
  14.8 6.6 %copy.29 = bf16[9,128,1024]{2,0,1:T(8,128)(2,1)} copy(bf16[9,128,1024]{1,2,0:T(8,128)(2,1)S(1)} %get-tuple-element.6) | data formatting | bytes 4718592 | tf_op jit(solution)/shard_map/convert_element_type | solution.py:141
  21.4 55.5 %all_to_all.32 = bf16[9,128,1024]{2,0,1:T(8,128)(2,1)} all-to-all(bf16[9,128,1024]{2,0,1:T(8,128)(2,1)} %copy.29), channel_id=1, replica_groups=mesh['var'=8,'tok'=32] {'var'}, dimensions={1} | all-to-all | bytes 4718592 | tf_op jit(solution)/shard_map/all_to_all | solution.py:142
  76.9 1.6 stack.2
  78.6 9.8 %all-to-all-start.1 = ((bf16[32,32,1024]{2,1,0:T(8,128)(2,1)}), bf16[32,32,1024]{2,1,0:T(8,128)(2,1)}, u32[]{:S(2)}, u32[]{:S(2)}) async-start(bf16[32,32,1024]{2,1,0:T(8,128)(2,1)} %stack.2), calls=%async_computation.1 | async-start | bytes 4194304 | tf_op jit(solution)/shard_map/all_to_all | solution.py:17
  89.6 5.1 %copy.31 = bf16[8,9,16,1024]{3,2,1,0:T(8,128)(2,1)} copy(bf16[8,9,16,1024]{3,1,2,0:T(8,128)(2,1)} %bitcast.119) | data formatting | bytes 4718592 | tf_op jit(solution)/shard_map/all_to_all | solution.py:142
  94.7 2.3 gather_fusion
  97.3 1.4 bitcast_select_fusion
  98.7 2.2 convolution_convert_fusion.3
  101.2 39.6 %all-to-all-done.1 = bf16[32,32,1024]{2,1,0:T(8,128)(2,1)} async-done(((bf16[32,32,1024]{2,1,0:T(8,128)(2,1)}), bf16[32,32,1024]{2,1,0:T(8,128)(2,1)}, u32[]{:S(2)}, u32[]{:S(2)}) %all-to-all-start.1) | async-done | bytes 2097184 | tf_op jit(solution)/shard_map/all_to_all | solution.py:17
  140.8 4.5 convolution_convert_fusion.1
  145.3 4.1 reshape.129
  149.5 23.7 %all-gather.3.cloned.1.call-done = bf16[1024,1024]{1,0:T(8,128)(2,1)} async-done(((bf16[32,1024]{1,0:T(8,128)(2,1)}), bf16[1024,1024]{1,0:T(8,128)(2,1)}) %all-gather.3.cloned.1.call-update) | async-done | bytes 2097168 | tf_op jit(solution)/shard_map/all_gather | solution.py:120
  173.1 5.0 %convolution_convert_fusion.2 = bf16[768,1024]{1,0:T(8,128)(2,1)} fusion(bf16[768,1024]{1,0:T(8,128)(2,1)} %bitcast_select_fusion, bf16[1024,1024]{1,0:T(8,128)(2,1)} %all-gather.3.cloned.1.call-done), kind=kOutput, calls=%fused_computation.32 | convolution fusion | flops 1611399168 | bytes 5242880 | tf_op jit(solution)/shard_map/dot_general | solution.py:48
  178.1 5.2 %reshape.126 = bf16[48,16,16,64]{3,2,1,0:T(8,128)(2,1)} reshape(bf16[768,1024]{1,0:T(8,128)(2,1)} %convolution_convert_fusion.2) | data formatting | bytes 3145728 | tf_op jit(solution)/shard_map/reshape | solution.py:50
  183.4 5.3 %fusion.12 = f32[16,1,48,16]{2,1,3,0:T(1,128)S(1)} fusion(bf16[16,64,1,1]{1,2,3,0:T(2,128)(2,1)S(1)} %reshape.159, bf16[48,16,16,64]{3,2,1,0:T(8,128)(2,1)} %reshape.126), kind=kOutput, calls=%fused_computation.19 | convolution fusion | flops 1572864 | bytes 1624064 | tf_op jit(solution)/shard_map/vthj,hj->tvh/dot_general | solution.py:58
  188.9 1.9 fusion.14
  191.4 3.8 mul.106
  195.3 6.3 %mul.107 = f32[768,1024]{1,0:T(8,128)} reshape(f32[48,16,16,64]{3,2,1,0:T(8,128)} %mul.106) | data formatting | bytes 6291456 | tf_op jit(solution)/shard_map/mul | solution.py:87
  202.5 3.3 multiply_convert_fusion
  205.9 3.2 convert_element_type.92
  209.0 4.5 fusion.22
  213.5 4.7 add_convert_fusion
  218.5 5.1 %scatter_fusion = bf16[72,16,1024]{2,1,0:T(8,128)(2,1)S(1)} fusion(bf16[72,16,1024]{2,1,0:T(8,128)(2,1)S(1)} %broadcast_in_dim.54, s32[48]{0:T(128)S(1)} %fusion.33, bf16[48,16,1024]{2,1,0:T(8,128)(2,1)} %bitcast.122), kind=kCustom, calls=%fused_computation.1 | custom fusion | bytes 4718784 | tf_op jit(solution)/shard_map/scatter | solution.py:147
  223.6 33.5 %all_to_all.33 = bf16[72,16,1024]{2,1,0:T(8,128)(2,1)S(1)} all-to-all(bf16[72,16,1024]{2,1,0:T(8,128)(2,1)S(1)} %scatter_fusion), channel_id=1, replica_groups=mesh['var'=8,'tok'=32] {'var'}, dimensions={0} | all-to-all | bytes 4718592 | tf_op jit(solution)/shard_map/all_to_all | solution.py:148
  257.6 2.9 copy.34
  260.5 6.1 %copy.35 = f32[9,128,1024]{1,2,0:T(8,128)} copy(f32[9,128,1024]{2,1,0:T(8,128)} %bitcast.118) | data formatting | bytes 9437184 | tf_op jit(solution)/shard_map/convert_element_type | solution.py:149
  266.5 6.8 %fusion.24 = f32[9,4,1024]{2,1,0:T(4,128)S(1)} fusion(bf16[9,4,128]{2,1,0:T(4,128)(2,1)S(1)} %copy-done.7, f32[9,128,1024]{1,2,0:T(8,128)} %copy.35, f32[9,1024,128]{2,1,0:T(8,128)} %get-tuple-element.7, f32[9,1024]{1,0:T(8,128)S(1)} %fusion.30), kind=kOutput, calls=%fused_computation.37 | convolution fusion | flops 68419584 | bytes 9630720 | tf_op jit(solution)/shard_map/spt,std->spd/dot_general | solution.py:150
  274.3 3.8 fusion.16
  278.3 1.0 convolution_convert_fusion.4
  279.3 187.7 %reduce-scatter.2.cloned.1.call-done = f32[9,128]{1,0:T(8,128)} async-done(((f32[9,4096]{1,0:T(8,128)}), f32[9,128]{1,0:T(8,128)}) %reduce-scatter.2.cloned.1.call-update) | async-done | bytes 4624 | tf_op jit(solution)/shard_map/reduce_scatter | solution.py:153
  (54 shorter events, 7.2 us)
Async XLA Ops:
  7.2 2.9 copy-start
  7.2 91.6 %all-gather.5.cloned.1.call-start = ((), (), s32[]{:S(2)}) async-start(), calls=%async_computation.5 | async-start | bytes 2162688 | tf_op jit(solution)/shard_map/all_gather | solution.py:123
  21.4 55.5 %copy-start.5 = (bf16[32,1024]{1,0:T(8,128)(2,1)S(1)}, bf16[32,1024]{1,0:T(8,128)(2,1)}, u32[]{:S(2)}) copy-start(bf16[32,1024]{1,0:T(8,128)(2,1)} %param.15) | copy-start | bytes 196612
  76.9 12.3 %copy-start.8 = (bf16[1024]{0:T(1024)(128)(2,1)S(1)}, bf16[1024]{0:T(1024)(128)(2,1)}, u32[]{:S(2)}) copy-start(bf16[1024]{0:T(1024)(128)(2,1)} %param.13) | copy-start | bytes 6148
  76.9 12.3 %copy-start.9 = (s32[72]{0:T(128)S(1)}, s32[72]{0:T(128)}, u32[]{:S(2)}) copy-start(s32[72]{0:T(128)} %param.10) | copy-start | bytes 868
  78.6 62.2 %all-to-all-start.1 = ((bf16[32,32,1024]{2,1,0:T(8,128)(2,1)}), bf16[32,32,1024]{2,1,0:T(8,128)(2,1)}, u32[]{:S(2)}, u32[]{:S(2)}) async-start(bf16[32,32,1024]{2,1,0:T(8,128)(2,1)} %stack.2), calls=%async_computation.1 | async-start | bytes 4194304 | tf_op jit(solution)/shard_map/all_to_all | solution.py:17
  88.4 84.7 %all-gather.3.cloned.1.call-start = ((), (), s32[]{:S(2)}) async-start(), calls=%async_computation.4 | async-start | bytes 2162688 | tf_op jit(solution)/shard_map/all_gather | solution.py:120
  89.2 377.9 %reduce-scatter.2.cloned.1.call-start = ((), (), s32[]{:S(2)}) async-start(), calls=%async_computation.6 | async-start | bytes 270336 | tf_op jit(solution)/shard_map/reduce_scatter | solution.py:153
  97.1 1.7 copy-start.6
  149.5 39.4 %copy-start.3 = (bf16[48,16,16,64]{3,2,1,0:T(8,128)(2,1)}, bf16[48,16,16,64]{3,2,1,0:T(8,128)(2,1)S(1)}, u32[]{:S(2)}) copy-start(bf16[48,16,16,64]{3,2,1,0:T(8,128)(2,1)S(1)} %reshape.129) | copy-start | bytes 4718596
  209.0 4.5 copy-start.4
  260.5 6.1 %copy-start.7 = (bf16[9,4,128]{2,1,0:T(4,128)(2,1)S(1)}, bf16[9,4,128]{2,1,0:T(4,128)(2,1)}, u32[]{:S(2)}) copy-start(bf16[9,4,128]{2,1,0:T(4,128)(2,1)} %param.9) | copy-start | bytes 27652
  273.4 4.9 %copy-start.2 = (bf16[1024,1024]{1,0:T(8,128)(2,1)S(1)}, bf16[1024,1024]{1,0:T(8,128)(2,1)}, u32[]{:S(2)}) copy-start(bf16[1024,1024]{1,0:T(8,128)(2,1)} %all-gather.5.cloned.1.call-done) | copy-start | bytes 6291460
  274.3 192.7 %copy-start.1 = (bf16[48,1024]{1,0:T(8,128)(2,1)S(1)}, bf16[48,1024]{1,0:T(8,128)(2,1)}, u32[]{:S(2)}) copy-start(bf16[48,1024]{1,0:T(8,128)(2,1)} %param.12) | copy-start | bytes 294916
Sparse Core Ops, SparseCore 0:
  10.6 80.9 all-gather.4
  94.1 78.9 all-gather.2
  274.4 192.5 reduce-scatter.1
